TPU v7x, 512 devices: a whole 4x4x16 slice. The times are simulated.
512 devices in a mesh: head: 8 (over x, core), group: 64 (over z, y).
Axes of the slice: x: 4, y: 4, z: 16, core: 2. Of those that a mesh axis runs over, the one named last changes fastest.
Arguments:
- query_proj: bfloat16 [8192, 2048], P('group', 'head'), may hold values from -6 to 6
- key_proj: bfloat16 [8192, 2048], P('group', 'head'), may hold values from -6 to 6
- value_proj: bfloat16 [8192, 4096], P('group', 'head'), may hold values from -6 to 6
- gate_proj: bfloat16 [8192, 4096], P('group', 'head'), may hold values from -6 to 6
- log_decay: float32 [8192, 8], P('group', 'head'), may hold values from -0.75 to 0
- out_weight: bfloat16 [4096, 2048], P('head'), may hold values from -0.09375 to 0.09375
- residual: bfloat16 [64, 128, 2048], P('group', 'head'), may hold values from -30 to 30
- norm_gain: float32 [2048], replicated, may hold values from 0.5 to 1.5
- vocab_weight: bfloat16 [49152, 2048], P(('head', 'group')), may hold values from -2 to 2
- targets: int32 [64, 128], P('group', 'head'), may hold values from 0 to 49151
- ref_logp: float32 [64, 128], P('group', 'head'), may hold values from -16 to -1
- response_mask: int32 [64, 128], P('group', 'head'), may hold values 0 or 1
- seq_lengths: int32 [32], replicated, may hold values from 1 to 4096, 8192 in all
Outputs:
- seq_ratio: float32 [32], replicated
- state_norms: float32 [64, 8], P('group', 'head')
- max_logits: float32 [64, 128], P('group', 'head')
Inputs may be any that keep to these rules, and one draw needn't show every extreme that they name: `seq_lengths`: the sequences lie end to end in order from position 0, the lengths summing to 8192.
All inputs are finite; a program needn't handle non-finite values. No bound on the sum of `response_mask` on one device may be relied on, other than what follows from the above.
Results may differ from a plain program's by a relative error of at most 0.00093.
Values may be sent and summed in bfloat16 or wider, within the bound.
No kernel may reach another device: no remote copies, remote signals or barrier semaphores. Data moves between devices by JAX's collectives and lax.ppermute only.
A program may use at most 192 MiB of HBM per device.

v0:
```python
import jax
import jax.numpy as jnp
from jax import lax
from jax.sharding import PartitionSpec as P


def entering(value, axis, combine, identity):
    size, index = (lax.axis_size(axis), lax.axis_index(axis))
    everything = jax.tree.map(lambda part: lax.all_gather(part, axis), value)
    start = jax.tree.map(
        lambda part, zero: jnp.broadcast_to(jnp.asarray(zero, part.dtype), part.shape),
        value,
        identity,
    )

    def lap(k, before):
        reached = k < index
        new = combine(before, jax.tree.map(lambda part: part[k], everything))
        return jax.tree.map(lambda a, b: jnp.where(reached, a, b), new, before)

    return lax.fori_loop(0, size, lap, start)


def merged_2(part, axis, combine):
    gathered = jax.tree.map(lambda a: lax.all_gather(a, axis), part)

    def take(source):
        return jax.tree.map(lambda a: lax.dynamic_index_in_dim(a, source, 0, False), gathered)

    return lax.fori_loop(
        1, lax.axis_size(axis), lambda source, state: combine(state, take(source)), take(0)
    )


def layer_norm(stream, width_eps):
    mean_val = jnp.mean(stream, axis=-1, keepdims=True)
    centered = stream - mean_val
    var_val = jnp.mean(centered * centered, axis=-1, keepdims=True)
    return centered / jnp.sqrt(var_val + width_eps)


def combine_state(earlier, later):
    decay_first, state_first = earlier
    decay_second, state_second = later
    return (decay_first * decay_second, decay_second[:, None, None] * state_first + state_second)


def combine_totals(first, second):
    max_first, sum_first, target_first = first
    max_second, sum_second, target_second = second
    top = jnp.maximum(max_first, max_second)
    merged = sum_first * jnp.exp(max_first - top) + sum_second * jnp.exp(max_second - top)
    return (top, merged, target_first + target_second)


def per_device(
    query_proj,
    key_proj,
    value_proj,
    gate_proj,
    log_decay,
    out_weight,
    residual,
    norm_gain,
    vocab_weight,
    targets,
    ref_logp,
    response_mask,
    seq_lengths,
):
    highest_precision = lax.Precision.HIGHEST
    head_count = lax.axis_size("head")
    group_count = lax.axis_size("group")
    head_index = lax.axis_index("head")
    group_index = lax.axis_index("group")
    tok_count = query_proj.shape[0]
    heads_here = log_decay.shape[1]
    key_width = query_proj.shape[1] // heads_here
    value_width = value_proj.shape[1] // heads_here
    slice_rows = residual.shape[1]
    seq_count = seq_lengths.shape[0]
    vocab_here = vocab_weight.shape[0]
    key_scaling = key_width ** (-0.5)
    starts = jnp.cumsum(seq_lengths) - seq_lengths
    local_pos = jnp.arange(tok_count, dtype=jnp.int32)
    positions = group_index * tok_count + local_pos
    seq_ids = jnp.sum((positions[:, None] >= starts[None, 1:]).astype(jnp.int32), axis=1)
    is_start = jnp.any(positions[:, None] == starts[None, :], axis=1)
    cumulative_decay = jnp.cumsum(log_decay, axis=0)
    same_seq = (seq_ids[:, None] == seq_ids[None, :]) & (local_pos[None, :] <= local_pos[:, None])
    gap_log = cumulative_decay[:, None, :] - cumulative_decay[None, :, :]
    decay_mat = jnp.where(same_seq[:, :, None], jnp.exp(jnp.minimum(gap_log, 0.0)), 0.0)
    query_heads = query_proj.reshape(tok_count, heads_here, key_width)
    key_heads = key_proj.reshape(tok_count, heads_here, key_width)
    value_heads = value_proj.reshape(tok_count, heads_here, value_width)
    raw_scores = jnp.einsum(
        "thd,shd->tsh", query_heads, key_heads, preferred_element_type=jnp.float32
    )
    weights_in = (raw_scores * key_scaling * decay_mat).astype(jnp.bfloat16)
    in_block = jnp.einsum(
        "tsh,shv->thv", weights_in, value_heads, preferred_element_type=jnp.float32
    )
    continuation_flags = (seq_ids == seq_ids[0]) & jnp.logical_not(is_start[0])
    final_decay_weight = jnp.where(
        (seq_ids == seq_ids[-1])[:, None],
        jnp.exp(cumulative_decay[-1][None, :] - cumulative_decay),
        0.0,
    )
    key_as_float = key_heads.astype(jnp.float32)
    value_as_float = value_heads.astype(jnp.float32)
    block_total_sum = jnp.einsum(
        "ane,anl->nel",
        key_as_float * final_decay_weight[:, :, None],
        value_as_float,
        precision=highest_precision,
    )
    block_decay = jnp.where(jnp.all(continuation_flags), jnp.exp(cumulative_decay[-1]), 0.0)
    decay_prefix, carried_state = entering(
        (block_decay, block_total_sum),
        "group",
        combine_state,
        (jnp.ones_like(block_decay), jnp.zeros_like(block_total_sum)),
    )
    query_as_float = query_heads.astype(jnp.float32)
    state_contribution = (
        jnp.einsum("ugo,gow->ugw", query_as_float, carried_state, precision=highest_precision)
        * key_scaling
        * (jnp.exp(cumulative_decay) * continuation_flags[:, None].astype(jnp.float32))[:, :, None]
    )
    retained = in_block + state_contribution
    state_norms = jnp.log(
        1.0 + jnp.sqrt(jnp.mean(carried_state * carried_state, axis=(1, 2)) + 1e-06)
    )[None, :]
    normed = layer_norm(retained, 1e-06)
    gate_float = gate_proj.reshape(tok_count, heads_here, value_width).astype(jnp.float32)
    gated_out = (
        (normed * jax.nn.silu(gate_float))
        .astype(jnp.bfloat16)
        .reshape(tok_count, heads_here * value_width)
    )
    full_branch = lax.psum(
        jnp.dot(gated_out, out_weight, preferred_element_type=jnp.float32), "head"
    )
    own_branch = lax.dynamic_slice_in_dim(full_branch, head_index * slice_rows, slice_rows, 0)
    stream = residual[0].astype(jnp.float32) + own_branch
    hidden = (layer_norm(stream, 1e-05) * norm_gain).astype(jnp.bfloat16)
    vocab_rows = lax.all_gather(vocab_weight, "head", axis=0, tiled=True)
    entry_ids = (
        (jnp.arange(head_count, dtype=jnp.int32)[:, None] * group_count + group_index) * vocab_here
        + jnp.arange(vocab_here, dtype=jnp.int32)[None, :]
    ).reshape(-1)
    all_targets = lax.all_gather(targets, "group", axis=0, tiled=True).reshape(-1)
    logits = lax.dot_general(
        lax.all_gather(hidden, "group", axis=0, tiled=True),
        vocab_rows,
        (((1,), (1,)), ((), ())),
        preferred_element_type=jnp.float32,
    )
    top = jnp.max(logits, axis=1)
    exp_total = jnp.sum(jnp.exp(logits - top[:, None]), axis=1)
    picked = jnp.sum(jnp.where(entry_ids[None, :] == all_targets[:, None], logits, 0.0), axis=1)
    merged_max, merged_total, merged_target = merged_2(
        (top, exp_total, picked), "group", combine_totals
    )
    own_start = group_index * slice_rows
    own_max = lax.dynamic_slice_in_dim(merged_max, own_start, slice_rows, 0)
    own_total = lax.dynamic_slice_in_dim(merged_total, own_start, slice_rows, 0)
    own_target = lax.dynamic_slice_in_dim(merged_target, own_start, slice_rows, 0)
    token_logp = own_target - own_max - jnp.log(own_total)
    token_ratio = response_mask[0].astype(jnp.float32) * (token_logp - ref_logp[0])
    own_positions = (
        group_index * tok_count + head_index * slice_rows + jnp.arange(slice_rows, dtype=jnp.int32)
    )
    own_seq = jnp.sum((own_positions[:, None] >= starts[None, 1:]).astype(jnp.int32), axis=1)
    member = (own_seq[:, None] == jnp.arange(seq_count, dtype=jnp.int32)[None, :]).astype(
        jnp.float32
    )
    partial_sums = jnp.sum(member * token_ratio[:, None], axis=0)
    seq_total = lax.psum(partial_sums, ("head", "group"))
    seq_ratio = seq_total / seq_lengths.astype(jnp.float32)
    return (seq_ratio, state_norms, own_max[None, :])


def solution(mesh):
    placed = (
        P("group", "head"),
        P("group", "head"),
        P("group", "head"),
        P("group", "head"),
        P("group", "head"),
        P("head", None),
        P("group", "head", None),
        P(),
        P(("head", "group"), None),
        P("group", "head"),
        P("group", "head"),
        P("group", "head"),
        P(),
    )
    return jax.shard_map(
        per_device,
        mesh=mesh,
        in_specs=placed,
        out_specs=(P(), P("group", "head"), P("group", "head")),
        check_vma=False,
    )
```

profile of v0, /device:TPU:1, one launch (start us, length us, event | category | flops | bytes accessed | tf_op | source)
XLA Modules:
  0.0 1104.0 jit_solution(7736796579347406270)
XLA Ops:
  11.4 2.0 select_multiply_fusion
  13.4 2.2 fusion.19
  20.4 124.9 %all-reduce = f32[64]{0:T(128)S(1)} all-reduce(f32[64]{0:T(128)S(1)} %fusion.38), channel_id=2, replica_groups=mesh['head'=8,'group'=64] {'group'}, use_global_device_ids=true, to_apply=%add | all-reduce | flops 64 | bytes 512
  146.7 167.5 %all-gather.14.cloned.1.call-done = f32[16384,512]{1,0:T(8,128)} async-done(((f32[256,512]{1,0:T(8,128)}), f32[16384,512]{1,0:T(8,128)}) %all-gather.14.cloned.1.call-update) | async-done | bytes 33554448 | tf_op jit(solution)/shard_map/all_gather | solution.py:9
  314.2 163.2 %while.34 = (s32[]{:T(128)}, f32[1,256,512]{2,1,0:T(8,128)S(1)}, s32[]{:T(128)}, f32[64,1]{0,1:T(1,128)S(1)}, f32[64,1,256,512]{3,2,1,0:T(8,128)}, /*index=5*/s32[]{:T(128)}, s32[]{:T(128)}) while((s32[]{:T(128)}, f32[1,256,512]{2,1,0:T(8,128)S(1)}, s32[]{:T(128)}, f32[64,1]{0,1:T(1,128)S(1)}, f32[64,1,256,512]{3,2,1,0:T(8,128)}, ...), condition=%wide.region_7.8_spmd.clone, body=%wide.region_6.7_spmd.clone.sunk | while | flops 524292 | bytes 1572981 | solution.py:21
  314.7 1.9 fusion.55
  317.3 1.9 fusion.55
  319.8 1.9 fusion.55
  322.4 1.9 fusion.55
  324.9 1.9 fusion.55
  327.5 1.9 fusion.55
  330.0 1.9 fusion.55
  332.6 1.9 fusion.55
  335.1 1.9 fusion.55
  337.7 1.9 fusion.55
  340.2 1.9 fusion.55
  342.8 1.9 fusion.55
  345.3 1.9 fusion.55
  347.9 1.9 fusion.55
  350.4 1.9 fusion.55
  353.0 1.9 fusion.55
  355.5 1.9 fusion.55
  358.1 1.9 fusion.55
  360.6 1.9 fusion.55
  363.2 1.9 fusion.55
  365.7 1.9 fusion.55
  368.3 1.9 fusion.55
  370.8 1.9 fusion.55
  373.4 1.9 fusion.55
  375.9 1.9 fusion.55
  378.5 1.9 fusion.55
  381.0 1.9 fusion.55
  383.6 1.9 fusion.55
  386.1 1.9 fusion.55
  388.7 1.9 fusion.55
  391.2 1.9 fusion.55
  393.8 1.9 fusion.55
  396.3 1.9 fusion.55
  398.9 1.9 fusion.55
  480.4 72.8 %all-reduce.3.cloned.1.call-done = f32[128,2048]{1,0:T(8,128)} async-done(((f32[128,2048]{1,0:T(8,128)}), f32[128,2048]{1,0:T(8,128)}) %all-reduce.3.cloned.1.call-update) | async-done | bytes 1048592 | tf_op jit(solution)/shard_map/psum | solution.py:141
  557.2 63.4 %all-gather.5 = s32[64,1,16]{2,1,0:T(1,128)S(1)} all-gather(s32[1,1,16]{2,1,0:T(1,128)S(1)} %bitcast.113), channel_id=1, replica_groups=mesh['head'=8,'group'=64] {'group'}, dimensions={0}, use_global_device_ids=true | all-gather | bytes 4160 | tf_op jit(solution)/shard_map/all_gather | solution.py:152
  623.5 107.8 %all-gather.10.cloned.1.call-done = bf16[1024,2048]{1,0:T(8,128)(2,1)} async-done(((bf16[16,2048]{1,0:T(8,128)(2,1)}), bf16[1024,2048]{1,0:T(8,128)(2,1)}) %all-gather.10.cloned.1.call-update) | async-done | bytes 4194320 | tf_op jit(solution)/shard_map/all_gather | solution.py:154
  731.3 6.2 fusion.45
  738.3 61.6 %all-gather.3 = f32[65536]{0:T(1024)S(1)} all-gather(f32[1024]{0:T(1024)S(1)} %get-tuple-element.318), channel_id=5, replica_groups=mesh['head'=8,'group'=64] {'group'}, dimensions={0}, use_global_device_ids=true | all-gather | bytes 266240 | tf_op jit(solution)/shard_map/all_gather | solution.py:25
  800.0 62.9 %all-gather.4 = f32[65536]{0:T(1024)S(1)} all-gather(f32[1024]{0:T(1024)S(1)} %get-tuple-element.317), channel_id=6, replica_groups=mesh['head'=8,'group'=64] {'group'}, dimensions={0}, use_global_device_ids=true | all-gather | bytes 266240 | tf_op jit(solution)/shard_map/all_gather | solution.py:25
  863.0 63.5 %all-gather.2 = f32[65536]{0:T(1024)S(1)} all-gather(f32[1024]{0:T(1024)S(1)} %get-tuple-element.355), channel_id=4, replica_groups=mesh['head'=8,'group'=64] {'group'}, dimensions={0}, use_global_device_ids=true | all-gather | bytes 266240 | tf_op jit(solution)/shard_map/all_gather | solution.py:25
  926.6 5.9 while.33
  933.3 162.6 %psum.15 = f32[32]{0:T(128)S(1)} all-reduce(f32[32]{0:T(128)S(1)} %select_reduce_fusion.1), channel_id=1, replica_groups=mesh['head'=8,'group'=64] {'head','group'}, use_global_device_ids=true, to_apply=%region_19.20 | all-reduce | flops 32 | bytes 256 | tf_op jit(solution)/shard_map/psum | solution.py:179
  (421 shorter events, 119.6 us)
Async XLA Ops:
  7.2 470.9 %copy-start = (bf16[512,2048]{1,0:T(8,128)(2,1)S(1)}, bf16[512,2048]{1,0:T(8,128)(2,1)}, u32[]{:S(2)}) copy-start(bf16[512,2048]{1,0:T(8,128)(2,1)} %param.22) | copy-start | bytes 6291460
  7.2 307.0 %all-gather.14.cloned.1.call-start = ((), (), s32[]{:S(2)}) async-start(), calls=%async_computation.3 | async-start | bytes 34078720 | tf_op jit(solution)/shard_map/all_gather | solution.py:9
  15.6 537.5 %all-reduce.3.cloned.1.call-start = ((), (), s32[]{:S(2)}) async-start(), calls=%async_computation | async-start | bytes 2097152 | tf_op jit(solution)/shard_map/psum | solution.py:141
  314.2 163.2 %copy-start.2 = (bf16[128,256]{1,0:T(8,128)(2,1)S(1)}, bf16[128,256]{1,0:T(8,128)(2,1)}, u32[]{:S(2)}) copy-start(bf16[128,256]{1,0:T(8,128)(2,1)} %param.17) | copy-start | bytes 196612
  314.2 163.9 %copy-start.8 = (bf16[128,512]{1,0:T(8,128)(2,1)S(1)}, bf16[128,512]{1,0:T(8,128)(2,1)}, u32[]{:S(2)}) copy-start(bf16[128,512]{1,0:T(8,128)(2,1)} %param.20) | copy-start | bytes 393220
  477.4 75.8 %copy-start.1 = (bf16[1,16,2048]{2,1,0:T(8,128)(2,1)S(1)}, bf16[1,16,2048]{2,1,0:T(8,128)(2,1)}, u32[]{:S(2)}) copy-start(bf16[1,16,2048]{2,1,0:T(8,128)(2,1)} %param.23) | copy-start | bytes 196612
  477.8 77.5 %copy-start.3 = (f32[2048]{0:T(1024)S(1)}, f32[2048]{0:T(1024)}, u32[]{:S(2)}) copy-start(f32[2048]{0:T(1024)} %param.24) | copy-start | bytes 24580
  478.0 79.2 %copy-start.4 = (s32[1,16]{1,0:T(1,128)S(1)}, s32[1,16]{1,0:T(1,128)}, u32[]{:S(2)}) copy-start(s32[1,16]{1,0:T(1,128)} %param.26) | copy-start | bytes 196
  479.6 143.9 %all-gather.12.cloned.1.call-start = ((), (), s32[]{:S(2)}) async-start(), calls=%async_computation.2 | async-start | bytes 3538944 | tf_op jit(solution)/shard_map/all_gather | solution.py:147
  480.4 251.0 %all-gather.10.cloned.1.call-start = ((), (), s32[]{:S(2)}) async-start(), calls=%async_computation.1 | async-start | bytes 4259840 | tf_op jit(solution)/shard_map/all_gather | solution.py:154
  737.5 195.0 %copy-start.6 = (f32[1,16]{1,0:T(1,128)S(1)}, f32[1,16]{1,0:T(1,128)}, u32[]{:S(2)}) copy-start(f32[1,16]{1,0:T(1,128)} %param.27) | copy-start | bytes 196
  737.6 195.0 %copy-start.7 = (s32[1,16]{1,0:T(1,128)S(1)}, s32[1,16]{1,0:T(1,128)}, u32[]{:S(2)}) copy-start(s32[1,16]{1,0:T(1,128)} %param.28) | copy-start | bytes 196
  737.6 358.3 %copy-start.5 = (s32[32]{0:T(128)S(1)}, s32[32]{0:T(128)}, u32[]{:S(2)}) copy-start(s32[32]{0:T(128)} %param.29) | copy-start | bytes 388
Sparse Core Ops, SparseCore 0:
  15.8 298.3 all-gather.13
  479.7 73.3 all-reduce.2
  555.3 36.6 all-gather.11
  594.8 136.4 all-gather.9
where the time goes:
time: 1110 us; the launch traced here: 1100 us
  blocking collectives  539 us (49%)
  waiting for transfers between devices  349 us (31%)
  other arithmetic  139 us (13%)
  local copies, waits for them, and re-layouts  44.2 us (4%)
  between operations  16.6 us (1%)
  matrix products  11.8 us (1%)
    all_gather x3, blocking collectives, merged_2(): gathered = jax.tree.map(lambda a: lax.all_gather(a, axis), part)  188 us
    all_gather x1, waiting for transfers between devices, entering(): everything = jax.tree.map(lambda part: lax.all_gather(part, axis), value)  167 us
    psum x1, blocking collectives, per_device(): seq_total = lax.psum(partial_sums, ('head', 'group'))  163 us
    unnamed x1, blocking collectives  125 us
    select_n x64, other arithmetic, lap(): return jax.tree.map(lambda a, b: jnp.where(reached, a, b), new, before)  125 us
    all_gather x1, waiting for transfers between devices, per_device(): lax.all_gather(hidden, 'group', axis=0, tiled=True)  108 us
    psum x1, waiting for transfers between devices, per_device(): lax.psum(jnp.dot(gated_out, out_weight, preferred_element_type=jnp.float3...  72.8 us
    all_gather x1, blocking collectives, per_device(): lax.all_gather(targets, 'group', axis=0, tiled=True).reshape(-1)  63.4 us
  transfers between devices with their start and end apart: 4, of which 3 were waited for; matrix products, arithmetic and copies ran while one was open for 1% of the time, Pallas kernels for 0%

commit v1 on v0

--- a/solution.py
+++ b/solution.py
@@ -1,7 +1,17 @@
+import functools
 import jax
 import jax.numpy as jnp
 from jax import lax
 from jax.sharding import PartitionSpec as P
+
+
+def remake_pipes_over_axis(field_in, across):
+    o_now = jnp.stack([field_in for _ in range(lax.axis_size(across))], axis=0)
+    far_arr = lax.all_to_all(o_now, axis_name=across, split_axis=0, concat_axis=0)
+    return jnp.concatenate(far_arr, axis=0)
+
+
+update_the_zones = functools.partial(remake_pipes_over_axis, across="group")
 
 
 def entering(value, axis, combine, identity):
@@ -151,7 +161,7 @@
     ).reshape(-1)
     all_targets = lax.all_gather(targets, "group", axis=0, tiled=True).reshape(-1)
     logits = lax.dot_general(
-        lax.all_gather(hidden, "group", axis=0, tiled=True),
+        update_the_zones(hidden),
         vocab_rows,
         (((1,), (1,)), ((), ())),
         preferred_element_type=jnp.float32,

time: 1110 us -> 1200 us (1.081)
  blocking collectives: 539 us -> 716 us
  waiting for transfers between devices: 349 us -> 242 us
  starting transfers between devices: 0.16 us -> 15.4 us
    all_gather x1, blocking collectives: 63.4 us -> 231 us  [per_device(): lax.all_gather(targets, 'group', axis=0, tiled=True).reshape(-1)]
    all_gather x1 -> x0, waiting for transfers between devices: 108 us -> none  [per_device(): lax.all_gather(hidden, 'group', axis=0, tiled=True)]
    all_to_all x0 -> x1, starting transfers between devices: none -> 15.3 us  [remake_pipes_over_axis(): lax.all_to_all(o_now, axis_name=across, split_axis=0, concat_axis=0)]
  transfers between devices with their start and end apart: 4 -> 4, of which waited for: 3 -> 2; matrix products, arithmetic and copies ran while one was open for 1% -> 1% of each run, Pallas kernels for 0% -> 0%
where the time goes in v1:
time: 1200 us; the launch traced here: 1190 us
  blocking collectives  716 us (60%)
  waiting for transfers between devices  242 us (20%)
  other arithmetic  139 us (12%)
  local copies, waits for them, and re-layouts  46.7 us (4%)
  between operations  16.6 us (1%)
  starting transfers between devices  15.4 us (1%)
    all_gather x1, blocking collectives, per_device(): lax.all_gather(targets, 'group', axis=0, tiled=True).reshape(-1)  231 us
    all_gather x3, blocking collectives, merged_2(): gathered = jax.tree.map(lambda a: lax.all_gather(a, axis), part)  188 us
    psum x1, blocking collectives, per_device(): seq_total = lax.psum(partial_sums, ('head', 'group'))  172 us
    all_gather x1, waiting for transfers between devices, entering(): everything = jax.tree.map(lambda part: lax.all_gather(part, axis), value)  167 us
    unnamed x1, blocking collectives  125 us
    select_n x64, other arithmetic, lap(): return jax.tree.map(lambda a, b: jnp.where(reached, a, b), new, before)  125 us
    psum x1, waiting for transfers between devices, per_device(): lax.psum(jnp.dot(gated_out, out_weight, preferred_element_type=jnp.float3...  73.5 us
    dynamic_slice x64, local copies, waits for them, and re-layouts, lap(): new = combine(before, jax.tree.map(lambda part: part[k], everything))  37.4 us
  transfers between devices with their start and end apart: 4, of which 2 were waited for; matrix products, arithmetic and copies ran while one was open for 1% of the time, Pallas kernels for 0%

profile of v1, /device:TPU:1, one launch (start us, length us, event | category | flops | bytes accessed | tf_op | source)
XLA Modules:
  0.0 1191.1 jit_solution(15771714421257359673)
XLA Ops:
  11.4 2.0 select_multiply_fusion
  13.4 2.2 fusion.19
  20.4 124.9 %all-reduce = f32[64]{0:T(128)S(1)} all-reduce(f32[64]{0:T(128)S(1)} %fusion.38), channel_id=2, replica_groups=mesh['head'=8,'group'=64] {'group'}, use_global_device_ids=true, to_apply=%add | all-reduce | flops 64 | bytes 512
  146.7 167.5 %all-gather.11.cloned.1.call-done = f32[16384,512]{1,0:T(8,128)} async-done(((f32[256,512]{1,0:T(8,128)}), f32[16384,512]{1,0:T(8,128)}) %all-gather.11.cloned.1.call-update) | async-done | bytes 33554448 | tf_op jit(solution)/shard_map/all_gather | solution.py:19
  314.2 163.2 %while.34 = (s32[]{:T(128)}, f32[1,256,512]{2,1,0:T(8,128)S(1)}, s32[]{:T(128)}, f32[64,1]{0,1:T(1,128)S(1)}, f32[64,1,256,512]{3,2,1,0:T(8,128)}, /*index=5*/s32[]{:T(128)}, s32[]{:T(128)}) while((s32[]{:T(128)}, f32[1,256,512]{2,1,0:T(8,128)S(1)}, s32[]{:T(128)}, f32[64,1]{0,1:T(1,128)S(1)}, f32[64,1,256,512]{3,2,1,0:T(8,128)}, ...), condition=%wide.region_7.8_spmd.clone, body=%wide.region_6.7_spmd.clone.sunk | while | flops 524292 | bytes 1572981 | solution.py:31
  314.7 1.9 fusion.55
  317.3 1.9 fusion.55
  319.8 1.9 fusion.55
  322.4 1.9 fusion.55
  324.9 1.9 fusion.55
  327.5 1.9 fusion.55
  330.0 1.9 fusion.55
  332.6 1.9 fusion.55
  335.1 1.9 fusion.55
  337.7 1.9 fusion.55
  340.2 1.9 fusion.55
  342.8 1.9 fusion.55
  345.3 1.9 fusion.55
  347.9 1.9 fusion.55
  350.4 1.9 fusion.55
  353.0 1.9 fusion.55
  355.5 1.9 fusion.55
  358.1 1.9 fusion.55
  360.6 1.9 fusion.55
  363.2 1.9 fusion.55
  365.7 1.9 fusion.55
  368.3 1.9 fusion.55
  370.8 1.9 fusion.55
  373.4 1.9 fusion.55
  375.9 1.9 fusion.55
  378.5 1.9 fusion.55
  381.0 1.9 fusion.55
  383.6 1.9 fusion.55
  386.1 1.9 fusion.55
  388.7 1.9 fusion.55
  391.2 1.9 fusion.55
  393.8 1.9 fusion.55
  396.3 1.9 fusion.55
  479.6 73.5 %all-reduce.3.cloned.1.call-done = f32[128,2048]{1,0:T(8,128)} async-done(((f32[128,2048]{1,0:T(8,128)}), f32[128,2048]{1,0:T(8,128)}) %all-reduce.3.cloned.1.call-update) | async-done | bytes 1048592 | tf_op jit(solution)/shard_map/psum | solution.py:151
  556.3 2.5 stack.2
  558.8 15.3 %all-to-all-start = ((bf16[64,16,2048]{2,1,0:T(8,128)(2,1)}), bf16[64,16,2048]{2,1,0:T(8,128)(2,1)}, u32[]{:S(2)}, u32[]{:S(2)}) async-start(bf16[64,16,2048]{2,1,0:T(8,128)(2,1)} %stack.2), calls=%async_computation | async-start | bytes 8388608 | tf_op jit(solution)/shard_map/all_to_all | solution.py:10
  575.0 231.2 %all-gather.5 = s32[64,1,16]{2,1,0:T(1,128)S(1)} all-gather(s32[1,1,16]{2,1,0:T(1,128)S(1)} %bitcast.114), channel_id=1, replica_groups=mesh['head'=8,'group'=64] {'group'}, dimensions={0}, use_global_device_ids=true | all-gather | bytes 4160 | tf_op jit(solution)/shard_map/all_gather | solution.py:162
  809.2 6.2 fusion.45
  816.2 62.3 %all-gather.3 = f32[65536]{0:T(1024)S(1)} all-gather(f32[1024]{0:T(1024)S(1)} %get-tuple-element.318), channel_id=5, replica_groups=mesh['head'=8,'group'=64] {'group'}, dimensions={0}, use_global_device_ids=true | all-gather | bytes 266240 | tf_op jit(solution)/shard_map/all_gather | solution.py:35
  878.6 63.2 %all-gather.4 = f32[65536]{0:T(1024)S(1)} all-gather(f32[1024]{0:T(1024)S(1)} %get-tuple-element.317), channel_id=6, replica_groups=mesh['head'=8,'group'=64] {'group'}, dimensions={0}, use_global_device_ids=true | all-gather | bytes 266240 | tf_op jit(solution)/shard_map/all_gather | solution.py:35
  941.8 62.5 %all-gather.2 = f32[65536]{0:T(1024)S(1)} all-gather(f32[1024]{0:T(1024)S(1)} %get-tuple-element.355), channel_id=4, replica_groups=mesh['head'=8,'group'=64] {'group'}, dimensions={0}, use_global_device_ids=true | all-gather | bytes 266240 | tf_op jit(solution)/shard_map/all_gather | solution.py:35
  1004.4 5.9 while.33
  1011.1 171.8 %psum.15 = f32[32]{0:T(128)S(1)} all-reduce(f32[32]{0:T(128)S(1)} %select_reduce_fusion.1), channel_id=1, replica_groups=mesh['head'=8,'group'=64] {'head','group'}, use_global_device_ids=true, to_apply=%region_19.20 | all-reduce | flops 32 | bytes 256 | tf_op jit(solution)/shard_map/psum | solution.py:189
  (421 shorter events, 120.9 us)
Async XLA Ops:
  7.2 470.9 %copy-start = (bf16[512,2048]{1,0:T(8,128)(2,1)S(1)}, bf16[512,2048]{1,0:T(8,128)(2,1)}, u32[]{:S(2)}) copy-start(bf16[512,2048]{1,0:T(8,128)(2,1)} %param.22) | copy-start | bytes 6291460
  7.2 307.0 %all-gather.11.cloned.1.call-start = ((), (), s32[]{:S(2)}) async-start(), calls=%async_computation.3 | async-start | bytes 34078720 | tf_op jit(solution)/shard_map/all_gather | solution.py:19
  15.6 537.5 %all-reduce.3.cloned.1.call-start = ((), (), s32[]{:S(2)}) async-start(), calls=%async_computation.1 | async-start | bytes 2097152 | tf_op jit(solution)/shard_map/psum | solution.py:151
  314.2 163.2 %copy-start.2 = (bf16[128,256]{1,0:T(8,128)(2,1)S(1)}, bf16[128,256]{1,0:T(8,128)(2,1)}, u32[]{:S(2)}) copy-start(bf16[128,256]{1,0:T(8,128)(2,1)} %param.17) | copy-start | bytes 196612
  314.2 163.9 %copy-start.8 = (bf16[128,512]{1,0:T(8,128)(2,1)S(1)}, bf16[128,512]{1,0:T(8,128)(2,1)}, u32[]{:S(2)}) copy-start(bf16[128,512]{1,0:T(8,128)(2,1)} %param.20) | copy-start | bytes 393220
  477.4 75.8 %copy-start.1 = (bf16[1,16,2048]{2,1,0:T(8,128)(2,1)S(1)}, bf16[1,16,2048]{2,1,0:T(8,128)(2,1)}, u32[]{:S(2)}) copy-start(bf16[1,16,2048]{2,1,0:T(8,128)(2,1)} %param.23) | copy-start | bytes 196612
  477.4 78.0 %copy-start.3 = (f32[2048]{0:T(1024)S(1)}, f32[2048]{0:T(1024)}, u32[]{:S(2)}) copy-start(f32[2048]{0:T(1024)} %param.24) | copy-start | bytes 24580
  558.8 16.2 %copy-start.4 = (s32[1,16]{1,0:T(1,128)S(1)}, s32[1,16]{1,0:T(1,128)}, u32[]{:S(2)}) copy-start(s32[1,16]{1,0:T(1,128)} %param.26) | copy-start | bytes 196
  558.8 250.4 %all-to-all-start = ((bf16[64,16,2048]{2,1,0:T(8,128)(2,1)}), bf16[64,16,2048]{2,1,0:T(8,128)(2,1)}, u32[]{:S(2)}, u32[]{:S(2)}) async-start(bf16[64,16,2048]{2,1,0:T(8,128)(2,1)} %stack.2), calls=%async_computation | async-start | bytes 8388608 | tf_op jit(solution)/shard_map/all_to_all | solution.py:10
  574.1 235.1 %all-gather.9.cloned.1.call-start = ((), (), s32[]{:S(2)}) async-start(), calls=%async_computation.2 | async-start | bytes 3538944 | tf_op jit(solution)/shard_map/all_gather | solution.py:157
  815.5 194.9 %copy-start.6 = (f32[1,16]{1,0:T(1,128)S(1)}, f32[1,16]{1,0:T(1,128)}, u32[]{:S(2)}) copy-start(f32[1,16]{1,0:T(1,128)} %param.27) | copy-start | bytes 196
  815.5 194.9 %copy-start.7 = (s32[1,16]{1,0:T(1,128)S(1)}, s32[1,16]{1,0:T(1,128)}, u32[]{:S(2)}) copy-start(s32[1,16]{1,0:T(1,128)} %param.28) | copy-start | bytes 196
  815.5 367.4 %copy-start.5 = (s32[32]{0:T(128)S(1)}, s32[32]{0:T(128)}, u32[]{:S(2)}) copy-start(s32[32]{0:T(128)} %param.29) | copy-start | bytes 388
Sparse Core Ops, SparseCore 0:
  15.8 298.3 all-gather.10
  479.8 73.3 all-reduce.2
  577.0 36.3 all-gather.8
